TPU v7x, 32 devices: a whole 2x2x4 slice. The times are simulated.
32 devices in a mesh: wl: 2 (over y), row: 16 (over z, x, core).
Axes of the slice: x: 2, y: 2, z: 4, core: 2. Of those that a mesh axis runs over, the one named last changes fastest.
Arguments:
- scenes: float32 [2, 4096, 4096], P(None, 'row'), may hold values from -6 to 6
- optics: bfloat16 [4, 2, 4096, 4096], P('wl', None, 'row'), may hold values from -4 to 4
- weights: float32 [4, 2], replicated, may hold values from 0.1 to 2
Outputs:
- blurred: float32 [2, 4096, 4096], P(None, 'row', 'wl')
All inputs are finite; a program needn't handle non-finite values.
Results may differ from a plain program's by a relative error of at most 0.0003.
Values may be sent and summed in bfloat16 or wider, within the bound.
No kernel may reach another device: no remote copies, remote signals or barrier semaphores. Data moves between devices by JAX's collectives and lax.ppermute only.
A program may use at most 128 MiB of HBM per device.

v0:
```python
import math
import jax
import jax.numpy as jnp
from jax import lax
from jax.sharding import PartitionSpec as P

PRECISE = lax.Precision.HIGHEST
NARROW = 32


def phase(left_ids, right_ids, modulus, orient):
    turns = (left_ids * right_ids % modulus).astype(jnp.float32)
    angles = turns * (orient * 2.0 * math.pi / modulus)
    return (jnp.cos(angles), jnp.sin(angles))


def ids(count):
    return jnp.arange(count, dtype=jnp.int32)


def cblock(cos_part, sin_part):
    return jnp.stack([jnp.stack([cos_part, -sin_part]), jnp.stack([sin_part, cos_part])])


def small_tables(out_count, in_count, modulus, orients):
    tables = []
    for orient in orients:
        cos_part, sin_part = phase(ids(out_count)[:, None], ids(in_count)[None, :], modulus, orient)
        tables.append(cblock(cos_part, sin_part))
    return jnp.stack(tables)


def twist(values, axis_e, cos_part, sin_part):
    real = jnp.take(values, 0, axis=axis_e)
    imag = jnp.take(values, 1, axis=axis_e)
    return jnp.stack([real * cos_part - imag * sin_part, real * sin_part + imag * cos_part], axis_e)


def canon_to_groups(canon, group_count):
    mcount, span_c = (canon.shape[0], canon.shape[-1] // 2)
    mid = canon.shape[1:-1]
    if group_count == mcount:
        return canon
    span = mcount * span_c // group_count
    flat = jnp.moveaxis(canon.reshape((mcount,) + mid + (2, span_c)), 0, -2)
    flat = flat.reshape(mid + (2, group_count, span))
    return jnp.moveaxis(flat, -2, 0).reshape((group_count,) + mid + (2 * span,))


def groups_to_canon(grouped, mcount, axis_g):
    group_count = grouped.shape[axis_g]
    if group_count == mcount:
        return grouped
    moved = jnp.moveaxis(grouped, axis_g, 0)
    mid = moved.shape[1:-1]
    span = moved.shape[-1] // 2
    span_c = group_count * span // mcount
    flat = jnp.moveaxis(moved.reshape((group_count,) + mid + (2, span)), 0, -2)
    flat = flat.reshape(mid + (2, mcount, span_c))
    canon = jnp.moveaxis(flat, -2, 0).reshape((mcount,) + mid + (2 * span_c,))
    return jnp.moveaxis(canon, 0, axis_g)


def forward_rows(scenes):
    rows_here, length = (scenes.shape[1], scenes.shape[2])
    across = length // NARROW
    half_k = across // 2
    grid = scenes.reshape((2, rows_here, NARROW, across))
    first_tab = jnp.transpose(small_tables(NARROW, NARROW, NARROW, (-1.0, 1.0)), (0, 3, 1, 2, 4))
    first = jnp.einsum("oaedb,drbn->oaern", first_tab, grid, precision=PRECISE)
    tw_cos, tw_sin = ([], [])
    for orient in (-1.0, 1.0):
        cos_part, sin_part = phase(ids(NARROW)[:, None], ids(across)[None, :], length, orient)
        tw_cos.append(cos_part)
        tw_sin.append(sin_part)
    tw_cos = jnp.stack(tw_cos)[:, :, None, :]
    tw_sin = jnp.stack(tw_sin)[:, :, None, :]
    turned = twist(first, 2, tw_cos, tw_sin)
    second_tab = jnp.transpose(small_tables(half_k, across, across, (-1.0, 1.0)), (0, 2, 4, 1, 3))
    second = jnp.einsum("oaern,oenfk->oarfk", turned, second_tab, precision=PRECISE)
    signs = 1.0 - 2.0 * (ids(across) % 2).astype(jnp.float32)
    nyquist = jnp.einsum("ern,n->er", first[0, 0], signs, precision=PRECISE)
    per_block = across // NARROW
    mcount = half_k // per_block
    blocks = second.reshape((2, NARROW, rows_here, 2, mcount, per_block))
    canon = jnp.transpose(blocks, (4, 3, 2, 0, 5, 1)).reshape((mcount, 2, rows_here, 2 * across))
    canon = canon.at[0, :, :, across].set(nyquist)
    return canon


def forward_cols(columns):
    length, width = (columns.shape[1], columns.shape[2])
    across = length // NARROW
    grid = columns.reshape((2, NARROW, across, width))
    first_tab = jnp.transpose(small_tables(NARROW, NARROW, NARROW, (-1.0, 1.0)), (0, 3, 1, 2, 4))
    first = jnp.einsum("oafeb,ebnj->oafnj", first_tab, grid, precision=PRECISE)
    tw_cos, tw_sin = ([], [])
    for orient in (-1.0, 1.0):
        cos_part, sin_part = phase(ids(NARROW)[:, None], ids(across)[None, :], length, orient)
        tw_cos.append(cos_part)
        tw_sin.append(sin_part)
    tw_cos = jnp.stack(tw_cos)[:, :, :, None]
    tw_sin = jnp.stack(tw_sin)[:, :, :, None]
    turned = twist(first, 2, tw_cos, tw_sin)
    second_tab = small_tables(across, across, across, (-1.0, 1.0))
    second = jnp.einsum("ofekn,oaenj->ofkaj", second_tab, turned, precision=PRECISE)
    return second.reshape((2, 2, length, width))


def inverse_cols_half(combined, group_count, half_index, part=0, parts=1):
    length, width = (combined.shape[1], combined.shape[2])
    across = length // NARROW
    grid = combined.reshape((2, NARROW, across, width))
    first_tab = jnp.transpose(small_tables(NARROW, NARROW, NARROW, (1.0,))[0], (2, 0, 1, 3))
    first = jnp.einsum("afeb,ebnj->afnj", first_tab, grid, precision=PRECISE)
    cos_part, sin_part = phase(ids(NARROW)[:, None], ids(across)[None, :], length, 1.0)
    turned = twist(first, 1, cos_part[:, :, None], sin_part[:, :, None])
    per_group = across // group_count
    per_half = per_group // 2
    per_part = per_half // parts
    k_ids = ids(per_part)[None, :] + part * per_part
    k_ids = ids(group_count)[:, None] * per_group + half_index * per_half + k_ids
    cos_k, sin_k = phase(k_ids.reshape((-1, 1)), ids(across)[None, :], across, 1.0)
    second_tab = jnp.transpose(cblock(cos_k, sin_k), (0, 2, 1, 3))
    second = jnp.einsum("fken,aenj->fkaj", second_tab, turned, precision=PRECISE)
    return second.reshape((2, group_count, per_part * NARROW, width))


def inverse_cols(combined):
    length, width = (combined.shape[1], combined.shape[2])
    across = length // NARROW
    grid = combined.reshape((2, NARROW, across, width))
    first_tab = jnp.transpose(small_tables(NARROW, NARROW, NARROW, (1.0,))[0], (2, 0, 1, 3))
    first = jnp.einsum("afeb,ebnj->afnj", first_tab, grid, precision=PRECISE)
    cos_part, sin_part = phase(ids(NARROW)[:, None], ids(across)[None, :], length, 1.0)
    turned = twist(first, 1, cos_part[:, :, None], sin_part[:, :, None])
    second_tab = jnp.transpose(small_tables(across, across, across, (1.0,))[0], (0, 2, 1, 3))
    second = jnp.einsum("fken,aenj->fkaj", second_tab, turned, precision=PRECISE)
    return second.reshape((2, length, width))


def inverse_rows(canon, length, scale, k_count=None, k_start=0):
    mcount, rows_here, width = (canon.shape[1], canon.shape[2], canon.shape[3])
    across = width // 2
    k_count = across if k_count is None else k_count
    first_tab = jnp.transpose(small_tables(NARROW, mcount, NARROW, (1.0, -1.0)), (0, 3, 1, 2, 4))
    first = jnp.einsum("oafem,emRj->oafRj", first_tab, canon, precision=PRECISE)
    lower = first[0, :, :, :, :across]
    upper = first[1, :, :, :, across:]
    flip_gain = -2.0 * (ids(NARROW) % 2).astype(jnp.float32)
    fix = flip_gain[:, None, None] * canon[:, 0, :, across][None]
    lane0 = (ids(across) == 0)[None, None, None, :]
    upper = jnp.where(lane0, upper + fix[..., None], upper)
    cos_up, sin_up = phase(ids(NARROW)[:, None], ids(across)[None, :], length, 1.0)
    cos_dn, sin_dn = phase(ids(NARROW)[:, None], ids(across)[None, :], length, -1.0)
    lower = twist(lower, 1, cos_up[:, None, :], sin_up[:, None, :])
    upper = twist(upper, 1, cos_dn[:, None, :], sin_dn[:, None, :])
    tabs = []
    for orient in (1.0, -1.0):
        k_ids = ids(k_count)[:, None] + k_start
        cos_part, sin_part = phase(k_ids, ids(across)[None, :], across, orient)
        tabs.append(cblock(cos_part, sin_part))
    tabs = jnp.transpose(jnp.stack(tabs) * scale, (0, 2, 4, 1, 3))
    out = jnp.einsum("aeRu,eufk->aRfk", lower, tabs[0], precision=PRECISE)
    out = out + jnp.einsum("aeRu,eufk->aRfk", upper, tabs[1], precision=PRECISE)
    return jnp.transpose(out, (2, 1, 3, 0)).reshape((2, rows_here, k_count * NARROW))


def pair_optics(optics):
    length = optics.shape[-1]
    across = length // NARROW
    half = length // 2
    mcount = half // across
    block = [lax.slice_in_dim(optics, across * i, across * (i + 1), axis=3) for i in range(NARROW)]
    windows = []
    for m in range(mcount):
        second = block[half // across if m == 0 else NARROW - m]
        windows.append(jnp.concatenate([block[NARROW - 1 - m], second], -1))
    windows = jnp.stack(windows)
    src = ids(2 * across)[:, None]
    dst = ids(across)[None, :]
    picker = jnp.logical_or(
        jnp.logical_and(src == across - dst, dst > 0), jnp.logical_and(src == across, dst == 0)
    ).astype(optics.dtype)
    mirrored = jnp.einsum("mwcpv,vu->mwcpu", windows, picker, preferred_element_type=jnp.float32)
    lower = jnp.stack(block[:mcount])
    return jnp.concatenate([lower, mirrored.astype(optics.dtype)], -1)


def local(scenes, optics, weights):
    row_count = lax.axis_size("row")
    length = scenes.shape[2]
    across = length // NARROW
    norm_factor = 1.0 / (float(length) * float(length))
    wl_index = lax.axis_index("wl")
    local_waves = optics.shape[0]
    weight_rows = lax.dynamic_slice_in_dim(weights, wl_index * local_waves, local_waves, 0)
    first_row = lax.axis_index("row") == 0
    wl_count = lax.axis_size("wl")
    rows_here = scenes.shape[1]
    own_rows = rows_here // wl_count
    if wl_count == 2 and own_rows * wl_count == rows_here:
        mine = lax.dynamic_slice_in_dim(scenes, wl_index * own_rows, own_rows, 1)
        canon = forward_rows(mine)
        mcount = canon.shape[0]
        sent = canon_to_groups(canon, row_count)
        got = lax.all_to_all(sent, "row", split_axis=0, concat_axis=2, tiled=True)[0]
        other = lax.ppermute(got, "wl", perm=[(0, 1), (1, 0)])
        got = got.reshape((2, row_count, own_rows, got.shape[-1]))
        other = other.reshape(got.shape)
        first_half = jnp.where(wl_index == 0, got, other)
        second_half = jnp.where(wl_index == 0, other, got)
        got = jnp.stack([first_half, second_half], 2).reshape((2, length, got.shape[-1]))
    else:
        canon = forward_rows(scenes)
        mcount = canon.shape[0]
        sent = canon_to_groups(canon, row_count)
        got = lax.all_to_all(sent, "row", split_axis=0, concat_axis=2, tiled=True)[0]
    spec = forward_cols(got)
    optic_canon = pair_optics(optics)
    optic_sent = canon_to_groups(optic_canon, row_count)
    optic_got = lax.all_to_all(optic_sent, "row", split_axis=0, concat_axis=3, tiled=True)[0]
    width = spec.shape[-1]
    span = width // 2
    lane_ids = ids(width)
    itself = jnp.logical_and(first_row, lane_ids % span == 0)
    direct = spec[0]
    flipped = spec[1]
    swapped = jnp.concatenate([flipped[..., span:], flipped[..., :span]], -1)
    partner = jnp.where(itself, flipped, swapped)
    mirror_real = partner[0]
    mirror_imag = -partner[1]
    even_real = 0.5 * (direct[0] + mirror_real)
    even_imag = 0.5 * (direct[1] + mirror_imag)
    odd_real = 0.5 * (direct[0] - mirror_real)
    odd_imag = 0.5 * (direct[1] - mirror_imag)
    combined_real = jnp.zeros_like(even_real)
    combined_imag = jnp.zeros_like(even_imag)
    for colour in range(local_waves):
        mixed_real = weight_rows[colour, 0] * even_real + weight_rows[colour, 1] * odd_real
        mixed_imag = weight_rows[colour, 0] * even_imag + weight_rows[colour, 1] * odd_imag
        resp_real = optic_got[colour, 0].astype(jnp.float32)
        resp_imag = optic_got[colour, 1].astype(jnp.float32)
        combined_real = combined_real + resp_real * mixed_real - resp_imag * mixed_imag
        combined_imag = combined_imag + resp_real * mixed_imag + resp_imag * mixed_real
    stacked = jnp.stack([combined_real, combined_imag])
    back = inverse_cols(stacked)
    if wl_count != 2 or own_rows * wl_count != rows_here:
        back = back.reshape((2, row_count, rows_here, width))
        returned = lax.all_to_all(back, "row", split_axis=1, concat_axis=1, tiled=True)
        returned = groups_to_canon(returned, mcount, 1)
        result_image = inverse_rows(returned, length, norm_factor)
        return lax.psum_scatter(result_image, "wl", scatter_dimension=2, tiled=True)
    per_group = across // row_count
    if per_group % 2 == 0 and per_group * row_count == across:
        parts = 4 if per_group % 8 == 0 else 1
        incoming = []
        for part in range(parts):
            given = inverse_cols_half(stacked, row_count, 1 - wl_index, part, parts)
            incoming.append(lax.ppermute(given, "wl", perm=[(0, 1), (1, 0)]))
        incoming = jnp.concatenate(incoming, 2)
        kept = inverse_cols_half(stacked, row_count, wl_index)
    else:
        back = back.reshape((2, row_count, 2, own_rows, width))
        kept = lax.dynamic_index_in_dim(back, wl_index, 2, keepdims=False)
        given = lax.dynamic_index_in_dim(back, 1 - wl_index, 2, keepdims=False)
        incoming = lax.ppermute(given, "wl", perm=[(0, 1), (1, 0)])
    summed = kept + incoming
    returned = lax.all_to_all(summed, "row", split_axis=1, concat_axis=1, tiled=True)
    returned = groups_to_canon(returned, mcount, 1)
    k_half = across // 2
    theirs = inverse_rows(returned, length, norm_factor, k_half, (1 - wl_index) * k_half)
    taken = lax.ppermute(theirs, "wl", perm=[(0, 1), (1, 0)])
    mine = inverse_rows(returned, length, norm_factor, k_half, wl_index * k_half)
    upper = jnp.where(wl_index == 0, mine, taken)
    lower = jnp.where(wl_index == 0, taken, mine)
    return jnp.concatenate([upper, lower], 1)


def solution(mesh):
    in_specs = (P(None, "row", None), P("wl", None, "row", None), P())
    out_specs = P(None, "row", "wl")
    return jax.shard_map(local, mesh=mesh, in_specs=in_specs, out_specs=out_specs, check_vma=False)
```

profile of v0, /device:TPU:10, one launch (start us, length us, event | category | flops | bytes accessed | tf_op | source)
XLA Modules:
  0.0 713.1 jit_solution(16438513354789603543)
XLA Ops:
  5.1 6.8 fusion.46
  15.1 13.9 %fusion.17 = f32[2,32,128,2,64,1]{2,4,5,3,1,0:T(8,128)S(1)} fusion(f32[2,32,2,128,128,1]{4,1,3,0,2,5:T(8,128)S(1)} %maximum_bitcast_fusion.1, f32[1,2,2,64,128]{4,3,2,1,0:T(8,128)S(1)} %maximum_bitcast_fusion.22, f32[1,2,2,64,128]{4,3,2,1,0:T(8,128)S(1)} %maximum_bitcast_fusion.21), kind=kOutput, calls=%fused_computation.26 | convolution fusion | flops 3221291008 | bytes 12845056 | tf_op jit(solution)/shard_map/oaern,oenfk->oarfk/dot_general | solution.py:80
  29.0 2.8 copy.170
  39.4 6.2 all-to-all-start.1
  45.7 3.7 fusion.232
  93.2 4.8 convolution_convert_fusion
  98.0 7.8 %pad_maximum_fusion = bf16[16,2,2,256,256]{3,4,2,1,0:T(8,128)(2,1)} fusion(bf16[16,2,2,256,128]{3,4,2,1,0:T(8,128)(2,1)} %convolution_convert_fusion, bf16[16,2,2,256,128]{3,4,2,1,0:T(8,128)(2,1)} %bitcast_dynamic-update-slice_fusion.15), kind=kLoop, calls=%fused_computation.5 | loop fusion | flops 16777216 | bytes 16777216 | tf_op jit(solution)/shard_map/concatenate | solution.py:187
  105.9 32.1 %all-to-all-done.1 = f32[16,2,128,256]{2,3,1,0:T(8,128)} async-done(((f32[16,2,128,256]{2,3,1,0:T(8,128)}), f32[16,2,128,256]{2,3,1,0:T(8,128)}, u32[]{:S(2)}, u32[]{:S(2)}) %all-to-all-start.1) | async-done | bytes 4194336 | tf_op jit(solution)/shard_map/all_to_all | solution.py:207
  138.0 5.4 all-to-all-start
  143.4 5.4 copy.172
  160.9 80.8 %collective-permute-done = f32[2,2048,256]{2,1,0:T(8,128)} collective-permute-done((f32[2,2048,256]{2,1,0:T(8,128)}, f32[2,2048,256]{2,1,0:T(8,128)}, u32[]{:S(2)}, u32[]{:S(2)}) %collective-permute-start) | collective-permute-done | bytes 4194336 | tf_op jit(solution)/shard_map/ppermute | solution.py:208
  241.7 5.3 copy.173
  247.0 4.1 bitcast_select_fusion.1
  251.1 3.9 pad_maximum_fusion.1
  255.0 13.3 %copy.175 = f32[2,16,2,128,256]{4,2,1,0,3:T(2,128)} copy(f32[2,16,2,128,256]{3,4,0,1,2:T(8,128)} %pad_maximum_fusion.1) | data formatting | bytes 16777216 | tf_op jit(solution)/shard_map/stack | solution.py:213
  268.3 10.9 %reshape.2175 = f32[2,32,128,256,1,1]{3,1,0,2,4,5:T(8,128)} reshape(f32[2,16,2,128,256]{4,2,1,0,3:T(2,128)} %copy.175) | data formatting | bytes 16777216 | tf_op jit(solution)/shard_map/reshape;reshape | solution.py:94
  279.2 16.7 %fusion.19 = f32[2,32,2,128,256]{4,1,3,2,0:T(8,128)S(1)} fusion(f32[2,32,128,256,1,1]{3,1,0,2,4,5:T(8,128)} %reshape.2175, f32[1,2,2,32,32]{4,3,2,1,0:T(8,128)S(1)} %fusion.98, f32[1,2,2,32,32]{4,3,2,1,0:T(8,128)S(1)} %maximum_bitcast_fusion.31), kind=kOutput, calls=%fused_computation.30 | convolution fusion | flops 3221233664 | bytes 25198592 | tf_op jit(solution)/shard_map/oafeb,ebnj->oafnj/dot_general | solution.py:96
  295.9 6.0 subtract_bitcast_fusion
  301.9 5.1 maximum_bitcast_fusion
  306.9 25.0 %fusion.22 = f32[2,2,128,32,256]{4,2,3,1,0:T(8,128)S(1)} fusion(f32[2,32,2,128,256,1]{4,1,3,0,2,5:T(8,128)S(1)} %maximum_bitcast_fusion, f32[1,2,2,128,128]{4,3,2,1,0:T(8,128)} %maximum_bitcast_fusion.12, f32[1,2,2,128,128]{4,3,2,1,0:T(8,128)} %maximum_bitcast_fusion.11), kind=kOutput, calls=%fused_computation.31 | convolution fusion | flops 12885032960 | bytes 34078720 | tf_op jit(solution)/shard_map/ofekn,oaenj->ofkaj/dot_general | solution.py:106
  331.9 5.8 copy-done.3
  337.8 4.3 slice.369
  342.1 8.2 %copy.181 = f32[1,2,128,32,256]{4,3,2,1,0:T(8,128)S(1)} copy(f32[1,2,128,32,256]{4,2,3,1,0:T(8,128)} %slice.369) | data formatting | bytes 16777216 | tf_op jit(solution)/shard_map/slice | solution.py:228
  350.3 4.0 fusion.230
  354.3 4.4 copy.180
  358.8 4.4 copy.182
  363.7 3.8 maximum_select_fusion
  367.5 11.5 %copy.166 = bf16[1,2,2,16,256,256]{5,4,3,2,1,0:T(8,128)(2,1)} copy(bf16[1,2,2,16,256,256]{4,5,2,1,3,0:T(8,128)(2,1)} %bitcast.54) | data formatting | bytes 16777216 | tf_op jit(solution)/shard_map/all_to_all | solution.py:222
  379.0 11.1 %fusion.32 = (f32[1,4096,256]{2,1,0:T(8,128)S(1)}, f32[1,4096,256]{2,1,0:T(8,128)S(1)}) fusion(bf16[2,2,4096,256]{3,2,1,0:T(8,128)(2,1)} %bitcast.577, f32[]{:T(128)} %bitcast.125, f32[]{:T(128)} %bitcast.124, f32[2,4096,256]{2,1,0:T(8,128)} %maximum_select_fusion, f32[1,1,128,32,256]{4,3,2,1,0:T(8,128)} %copy.180, f32[]{:T(128)} %bitcast.130, f32[]{:T(128)} %bitcast.129, ...), kind=kLoop, calls=%fused_computation.49 | loop fusion | flops 36700160 | bytes 33554448 | tf_op jit(solution)/shard_map/sub | solution.py:244
  395.0 7.7 %fusion.47 = f32[32,2,128,256]{3,0,2,1:T(8,128)S(1)} fusion(f32[1,32,128,256]{3,1,0,2:T(8,128)S(1)} %copy.184, f32[1,32,128,256]{3,1,0,2:T(8,128)S(1)} %copy.183, f32[1,2,32,32]{3,2,1,0:T(8,128)S(1)} %copy-done.17, f32[1,2,32,32]{3,2,1,0:T(8,128)S(1)} %copy-done.15), kind=kOutput, calls=%fused_computation.90 | convolution fusion | flops 1612713984 | bytes 16793600 | tf_op jit(solution)/shard_map/afeb,ebnj->afnj/dot_general | solution.py:115
  405.9 9.4 %fusion.57 = f32[2,16,32,256]{3,1,2,0:T(8,128)S(1)} fusion(f32[32,2,128,256]{3,0,2,1:T(8,128)S(1)} %pad_maximum_fusion.2, f32[1,2,16,128]{3,2,1,0:T(8,128)S(1)} %copy-done.25, f32[1,2,16,128]{3,2,1,0:T(8,128)S(1)} %copy-done.24), kind=kOutput, calls=%fused_computation.111 | convolution fusion | flops 805314560 | bytes 9469952 | tf_op jit(solution)/shard_map/fken,aenj->fkaj/dot_general | solution.py:125
  416.8 10.7 %fusion.60 = f32[2,16,32,256]{3,1,2,0:T(8,128)} fusion(f32[32,2,128,256]{3,0,2,1:T(8,128)S(1)} %pad_maximum_fusion.2, f32[1,2,16,128]{3,2,1,0:T(8,128)S(1)} %copy-done.27, f32[1,2,16,128]{3,2,1,0:T(8,128)S(1)} %copy-done.26), kind=kOutput, calls=%fused_computation.112 | convolution fusion | flops 805314560 | bytes 9469952 | tf_op jit(solution)/shard_map/fken,aenj->fkaj/dot_general | solution.py:125
  428.1 10.5 %fusion.63 = f32[2,16,32,256]{3,1,2,0:T(8,128)} fusion(f32[32,2,128,256]{3,0,2,1:T(8,128)S(1)} %pad_maximum_fusion.2, f32[1,2,16,128]{3,2,1,0:T(8,128)S(1)} %copy-done.29, f32[1,2,16,128]{3,2,1,0:T(8,128)S(1)} %copy-done.28), kind=kOutput, calls=%fused_computation.113 | convolution fusion | flops 805314560 | bytes 9469952 | tf_op jit(solution)/shard_map/fken,aenj->fkaj/dot_general | solution.py:125
  440.1 10.5 %fusion.66 = f32[2,16,32,256]{3,1,2,0:T(8,128)} fusion(f32[32,2,128,256]{3,0,2,1:T(8,128)S(1)} %pad_maximum_fusion.2, f32[1,2,16,128]{3,2,1,0:T(8,128)S(1)} %copy-done.31, f32[1,2,16,128]{3,2,1,0:T(8,128)S(1)} %copy-done.30), kind=kOutput, calls=%fused_computation.114 | convolution fusion | flops 805314560 | bytes 9469952 | tf_op jit(solution)/shard_map/fken,aenj->fkaj/dot_general | solution.py:125
  451.6 13.0 %fusion.48 = f32[2,64,32,256]{3,1,2,0:T(8,128)S(1)} fusion(f32[32,2,128,256]{3,0,2,1:T(8,128)} %copy-done.2, f32[1,2,64,128]{3,2,1,0:T(8,128)S(1)} %get-tuple-element.164, f32[1,2,64,128]{3,2,1,0:T(8,128)S(1)} %get-tuple-element.163), kind=kOutput, calls=%fused_computation.92 | convolution fusion | flops 3221258240 | bytes 12713984 | tf_op jit(solution)/shard_map/fken,aenj->fkaj/dot_general | solution.py:125
  467.1 19.4 %collective-permute-done.3 = f32[2,16,32,256]{3,1,2,0:T(8,128)} collective-permute-done((f32[2,16,32,256]{3,1,2,0:T(8,128)}, f32[2,16,32,256]{3,1,2,0:T(8,128)}, u32[]{:S(2)}, u32[]{:S(2)}) %collective-permute-start.3) | collective-permute-done | bytes 1048608 | tf_op jit(solution)/shard_map/ppermute | solution.py:260
  486.5 20.7 %collective-permute-done.4 = f32[2,16,32,256]{3,1,2,0:T(8,128)} collective-permute-done((f32[2,16,32,256]{3,1,2,0:T(8,128)}, f32[2,16,32,256]{3,1,2,0:T(8,128)}, u32[]{:S(2)}, u32[]{:S(2)}) %collective-permute-start.4) | collective-permute-done | bytes 1048608 | tf_op jit(solution)/shard_map/ppermute | solution.py:260
  507.2 6.0 maximum_add_fusion
  513.2 4.4 copy.194
  517.7 6.0 all-to-all-start.2
  524.6 91.5 %all-to-all-done.2 = f32[2,16,128,256]{3,2,0,1:T(8,128)} async-done(((f32[2,16,128,256]{3,2,0,1:T(8,128)}), f32[2,16,128,256]{3,2,0,1:T(8,128)}, u32[]{:S(2)}, u32[]{:S(2)}) %all-to-all-start.2) | async-done | bytes 4194336 | tf_op jit(solution)/shard_map/all_to_all | solution.py:269
  616.0 18.1 %convolution_bitcast_fusion = f32[2,32,2,128,256]{4,1,3,2,0:T(8,128)S(1)} fusion(f32[2,16,128,256,1,1]{3,2,0,1,5,4:T(8,128)} %bitcast.181, f32[1,2,2,32,16]{3,4,2,1,0:T(8,128)S(1)} %maximum_bitcast_fusion.45, f32[1,2,2,32,16]{3,4,2,1,0:T(8,128)S(1)} %maximum_bitcast_fusion.44), kind=kOutput, calls=%fused_computation.32 | convolution fusion | flops 1610616832 | bytes 20987904 | tf_op jit(solution)/shard_map/oafem,emRj->oafRj/dot_general | solution.py:147
  639.9 6.9 fusion.38
  646.8 7.1 fusion.51
  657.2 8.1 %fusion.40 = f32[32,128,2,64,1]{1,3,4,2,0:T(8,128)S(1)} fusion(f32[32,2,128,128,1]{3,0,2,1,4:T(8,128)} %copy-done.6, f32[2,2,128,2,64]{2,4,1,3,0:T(8,128)S(1)} %fusion.75), kind=kOutput, calls=%fused_computation.83 | convolution fusion | flops 1610612736 | bytes 6422528 | tf_op jit(solution)/shard_map/aeRu,eufk->aRfk/dot_general | solution.py:165
  665.3 6.9 fusion.52
  673.4 29.8 %collective-permute-done.5 = f32[2,128,2048]{1,2,0:T(8,128)} collective-permute-done((f32[2,128,2048]{1,2,0:T(8,128)S(1)}, f32[2,128,2048]{1,2,0:T(8,128)}, u32[]{:S(2)}, u32[]{:S(2)}) %collective-permute-start.5) | collective-permute-done | bytes 2097184 | tf_op jit(solution)/shard_map/ppermute | solution.py:273
  707.4 5.3 copy.202
  (232 shorter events, 99.4 us)
Async XLA Ops:
  0.0 150.5 %copy-start = (f32[4,2]{0,1:T(2,128)S(1)}, f32[4,2]{0,1:T(2,128)}, u32[]{:S(2)}) copy-start(f32[4,2]{0,1:T(2,128)} %param.23) | copy-start | bytes 100
  4.5 0.6 copy-start.14
  4.5 0.6 copy-start.16
  12.1 1.9 copy-start.10
  12.1 1.9 copy-start.12
  29.0 3.5 copy-start.35
  31.9 2.8 copy-start.7
  39.4 98.6 %all-to-all-start.1 = ((f32[16,2,128,256]{2,3,1,0:T(8,128)}), f32[16,2,128,256]{2,3,1,0:T(8,128)}, u32[]{:S(2)}, u32[]{:S(2)}) async-start(f32[16,2,128,256]{2,3,1,0:T(8,128)} %scatter.4), calls=%async_computation.1 | async-start | bytes 8388608 | tf_op jit(solution)/shard_map/all_to_all | solution.py:207
  45.7 47.5 %copy-start.32 = (pred[128]{0:T(512)(128)(4,1)}, pred[128]{0:T(512)(128)(4,1)S(1)}, u32[]{:S(2)}) copy-start(pred[128]{0:T(512)(128)(4,1)S(1)} %get-tuple-element.218) | copy-start | bytes 388
  57.3 8.8 %copy-start.8 = (bf16[2,2,256,128]{3,2,1,0:T(8,128)(2,1)S(1)}, bf16[2,2,256,128]{3,2,1,0:T(8,128)(2,1)}, u32[]{:S(2)}) copy-start(bf16[2,2,256,128]{3,2,1,0:T(8,128)(2,1)} %get-tuple-element.143) | copy-start | bytes 786436
  63.7 2.4 copy-start.9
  84.5 8.7 %copy-start.34 = (s32[128]{0:T(128)S(1)}, s32[128]{0:T(128)}, u32[]{:S(2)}) copy-start(s32[128]{0:T(128)} %iota_subtract_fusion) | copy-start | bytes 1540
  138.0 229.5 %all-to-all-start = ((bf16[16,2,2,256,256]{3,4,2,1,0:T(8,128)(2,1)}), bf16[16,2,2,256,256]{3,4,2,1,0:T(8,128)(2,1)}, u32[]{:S(2)}, u32[]{:S(2)}) async-start(bf16[16,2,2,256,256]{3,4,2,1,0:T(8,128)(2,1)} %pad_maximum_fusion), calls=%async_computation | async-start | bytes 16777216 | tf_op jit(solution)/shard_map/all_to_all | solution.py:222
  143.4 6.9 copy-start.13
  143.4 7.0 copy-start.11
  148.7 92.9 %collective-permute-start = (f32[2,2048,256]{2,1,0:T(8,128)}, f32[2,2048,256]{2,1,0:T(8,128)}, u32[]{:S(2)}, u32[]{:S(2)}) collective-permute-start(f32[2,2048,256]{2,1,0:T(8,128)} %bitcast.586), channel_id=1, source_target_pairs={{0,16},{16,0},{1,17},{17,1},{2,18},{18,2},{3,19},{19,3},{4,20},{20... | collective-permute-start | bytes 12582920 | tf_op jit(solution)/shard_map/ppermute | solution.py:208
  153.8 5.6 copy-start.20
  153.8 5.6 copy-start.22
  331.9 5.8 copy-start.3
  392.5 2.5 copy-start.15
  392.5 2.5 copy-start.17
  395.0 7.7 %copy-start.18 = (f32[32,128]{0,1:T(8,128)S(1)}, f32[32,128]{0,1:T(8,128)}, u32[]{:S(2)}) copy-start(f32[32,128]{0,1:T(8,128)} %copy.185) | copy-start | bytes 49156
  395.0 7.7 %copy-start.19 = (f32[32,128]{0,1:T(8,128)S(1)}, f32[32,128]{0,1:T(8,128)}, u32[]{:S(2)}) copy-start(f32[32,128]{0,1:T(8,128)} %copy.186) | copy-start | bytes 49156
  404.1 1.7 copy-start.24
  404.2 1.7 copy-start.25
  405.8 34.3 %copy-start.2 = (f32[32,2,128,256]{3,0,2,1:T(8,128)}, f32[32,2,128,256]{3,0,2,1:T(8,128)S(1)}, u32[]{:S(2)}) copy-start(f32[32,2,128,256]{3,0,2,1:T(8,128)S(1)} %pad_maximum_fusion.2) | copy-start | bytes 25165828
  405.9 11.0 %copy-start.26 = (f32[1,2,16,128]{3,2,1,0:T(8,128)S(1)}, f32[1,2,16,128]{3,2,1,0:T(8,128)}, u32[]{:S(2)}) copy-start(f32[1,2,16,128]{3,2,1,0:T(8,128)} %get-tuple-element.179) | copy-start | bytes 49156
  405.9 11.0 %copy-start.27 = (f32[1,2,16,128]{3,2,1,0:T(8,128)S(1)}, f32[1,2,16,128]{3,2,1,0:T(8,128)}, u32[]{:S(2)}) copy-start(f32[1,2,16,128]{3,2,1,0:T(8,128)} %get-tuple-element.180) | copy-start | bytes 49156
  415.2 51.8 %collective-permute-start.1 = (f32[2,16,32,256]{3,1,2,0:T(8,128)S(1)}, f32[2,16,32,256]{3,1,2,0:T(8,128)S(1)}, u32[]{:S(2)}, u32[]{:S(2)}) collective-permute-start(f32[2,16,32,256]{3,1,2,0:T(8,128)S(1)} %fusion.57), channel_id=1, source_target_pairs={{0,16},{16,0},{1,17},{17,1},{2,18},{18,2},{3,19},{19,3},{4,20},{20... | collective-permute-start | bytes 3145736 | tf_op jit(solution)/shard_map/ppermute | solution.py:260
  416.8 11.3 %copy-start.28 = (f32[1,2,16,128]{3,2,1,0:T(8,128)S(1)}, f32[1,2,16,128]{3,2,1,0:T(8,128)}, u32[]{:S(2)}) copy-start(f32[1,2,16,128]{3,2,1,0:T(8,128)} %get-tuple-element.181) | copy-start | bytes 49156
  416.8 11.3 %copy-start.29 = (f32[1,2,16,128]{3,2,1,0:T(8,128)S(1)}, f32[1,2,16,128]{3,2,1,0:T(8,128)}, u32[]{:S(2)}) copy-start(f32[1,2,16,128]{3,2,1,0:T(8,128)} %get-tuple-element.182) | copy-start | bytes 49156
  427.6 39.5 %collective-permute-start.2 = (f32[2,16,32,256]{3,1,2,0:T(8,128)}, f32[2,16,32,256]{3,1,2,0:T(8,128)S(1)}, u32[]{:S(2)}, u32[]{:S(2)}) collective-permute-start(f32[2,16,32,256]{3,1,2,0:T(8,128)} %fusion.60), channel_id=1, source_target_pairs={{0,16},{16,0},{1,17},{17,1},{2,18},{18,2},{3,19},{19,3},{4,20},{20... | collective-permute-start | bytes 3145736 | tf_op jit(solution)/shard_map/ppermute | solution.py:260
  428.1 12.0 %copy-start.30 = (f32[1,2,16,128]{3,2,1,0:T(8,128)S(1)}, f32[1,2,16,128]{3,2,1,0:T(8,128)}, u32[]{:S(2)}) copy-start(f32[1,2,16,128]{3,2,1,0:T(8,128)} %get-tuple-element.183) | copy-start | bytes 49156
  428.1 12.0 %copy-start.31 = (f32[1,2,16,128]{3,2,1,0:T(8,128)S(1)}, f32[1,2,16,128]{3,2,1,0:T(8,128)}, u32[]{:S(2)}) copy-start(f32[1,2,16,128]{3,2,1,0:T(8,128)} %get-tuple-element.184) | copy-start | bytes 49156
  438.6 47.9 %collective-permute-start.3 = (f32[2,16,32,256]{3,1,2,0:T(8,128)}, f32[2,16,32,256]{3,1,2,0:T(8,128)}, u32[]{:S(2)}, u32[]{:S(2)}) collective-permute-start(f32[2,16,32,256]{3,1,2,0:T(8,128)} %fusion.63), channel_id=1, source_target_pairs={{0,16},{16,0},{1,17},{17,1},{2,18},{18,2},{3,19},{19,3},{4,20},{20... | collective-permute-start | bytes 3145736 | tf_op jit(solution)/shard_map/ppermute | solution.py:260
  450.6 56.6 %collective-permute-start.4 = (f32[2,16,32,256]{3,1,2,0:T(8,128)}, f32[2,16,32,256]{3,1,2,0:T(8,128)}, u32[]{:S(2)}, u32[]{:S(2)}) collective-permute-start(f32[2,16,32,256]{3,1,2,0:T(8,128)} %fusion.66), channel_id=1, source_target_pairs={{0,16},{16,0},{1,17},{17,1},{2,18},{18,2},{3,19},{19,3},{4,20},{20... | collective-permute-start | bytes 3145736 | tf_op jit(solution)/shard_map/ppermute | solution.py:260
  517.7 98.3 %all-to-all-start.2 = ((f32[2,16,128,256]{3,2,0,1:T(8,128)}), f32[2,16,128,256]{3,2,0,1:T(8,128)}, u32[]{:S(2)}, u32[]{:S(2)}) async-start(f32[2,16,128,256]{3,2,0,1:T(8,128)} %copy.194), calls=%async_computation.2 | async-start | bytes 8388608 | tf_op jit(solution)/shard_map/all_to_all | solution.py:269
  634.2 0.7 copy-start.21
  634.2 0.7 copy-start.23
  634.9 1.8 copy-start.33
  638.8 8.1 %copy-start.4 = (f32[32,2,128,128,1]{3,0,2,1,4:T(8,128)}, f32[32,2,128,128,1]{3,0,2,1,4:T(8,128)S(1)}, u32[]{:S(2)}) copy-start(f32[32,2,128,128,1]{3,0,2,1,4:T(8,128)S(1)} %maximum_bitcast_fusion.4) | copy-start | bytes 12582916
  639.9 14.0 %copy-start.6 = (f32[32,2,128,128,1]{3,0,2,1,4:T(8,128)}, f32[32,2,128,128,1]{3,0,2,1,4:T(8,128)S(1)}, u32[]{:S(2)}) copy-start(f32[32,2,128,128,1]{3,0,2,1,4:T(8,128)S(1)} %maximum_bitcast_fusion.5) | copy-start | bytes 12582916
  655.2 48.0 %collective-permute-start.5 = (f32[2,128,2048]{1,2,0:T(8,128)S(1)}, f32[2,128,2048]{1,2,0:T(8,128)}, u32[]{:S(2)}, u32[]{:S(2)}) collective-permute-start(f32[2,128,2048]{1,2,0:T(8,128)S(1)} %bitcast.587), channel_id=1, source_target_pairs={{0,16},{16,0},{1,17},{17,1},{2,18},{18,2},{3,19},{19,3},{4,20},{20... | collective-permute-start | bytes 6291464 | tf_op jit(solution)/shard_map/ppermute | solution.py:273
  656.8 8.5 %copy-start.5 = (f32[32,2,128,128,1]{3,0,2,1,4:T(8,128)S(1)}, f32[32,2,128,128,1]{3,0,2,1,4:T(8,128)}, u32[]{:S(2)}) copy-start(f32[32,2,128,128,1]{3,0,2,1,4:T(8,128)} %copy-done.4) | copy-start | bytes 12582916
  705.1 7.7 %copy-start.1 = (f32[4,2]{0,1:T(2,128)S(1)}, f32[4,2]{0,1:T(2,128)}, u32[]{:S(2)}) copy-start(f32[4,2]{0,1:T(2,128)} %param.23) | copy-start | bytes 100
where the time goes:
time: 724 us; the launch traced here: 713 us
  waiting for transfers between devices  274 us (38%)
  matrix products  178 us (25%)
  local copies, waits for them, and re-layouts  159 us (22%)
  other arithmetic  72.8 us (10%)
  starting transfers between devices  24.9 us (3%)
    all_to_all x1, waiting for transfers between devices, local(): lax.all_to_all(summed, 'row', split_axis=1, concat_axis=1, tiled=True)  91.5 us
    ppermute x1, waiting for transfers between devices, local(): other = lax.ppermute(got, 'wl', perm=[(0, 1), (1, 0)])  80.8 us
    dot_general x5, matrix products, inverse_cols_half(): jnp.einsum('fken,aenj->fkaj', second_tab, turned, precision=PRECISE)  54.1 us
    unnamed x118, local copies, waits for them, and re-layouts  48.7 us
    ppermute x4, waiting for transfers between devices, local(): incoming.append(lax.ppermute(given, 'wl', perm=[(0, 1), (1, 0)]))  40.1 us
    all_to_all x1, waiting for transfers between devices, local(): lax.all_to_all(sent, 'row', split_axis=0, concat_axis=2, tiled=True)[0]  32.1 us
    ppermute x1, waiting for transfers between devices, local(): taken = lax.ppermute(theirs, 'wl', perm=[(0, 1), (1, 0)])  29.8 us
    dot_general x1, matrix products, forward_cols(): jnp.einsum('ofekn,oaenj->ofkaj', second_tab, turned, precision=PRECISE)  25 us
  transfers between devices with their start and end apart: 9, of which 6 were waited for; matrix products, arithmetic and copies ran while one was open for 36% of the time, Pallas kernels for 0%

commit v1 on v0

--- a/solution.py
+++ b/solution.py
@@ -6,6 +6,29 @@
 
 PRECISE = lax.Precision.HIGHEST
 NARROW = 32
+
+
+def split_up(x, dim, devices):
+    dims = x.shape
+    parts = x.reshape(*dims[:dim], devices, dims[dim] // devices, *dims[dim + 1 :])
+    return jnp.moveaxis(parts, dim, 0)
+
+
+def in_order(blocks, dim):
+    blocks = jnp.moveaxis(blocks, 0, dim)
+    lengths = blocks.shape
+    return blocks.reshape(*lengths[:dim], lengths[dim] * lengths[dim + 1], *lengths[dim + 2 :])
+
+
+def exchange_directly(array, axis, split_dim, concat_dim):
+    size, position = (lax.axis_size(axis), lax.axis_index(axis))
+    tiles = split_up(array, split_dim, size)
+    gathered = [tiles[position]]
+    for lap in range(1, size):
+        sent = tiles[(position + lap) % size]
+        gathered.append(lax.ppermute(sent, axis, [(i, (i + lap) % size) for i in range(size)]))
+    tiles = jnp.stack(gathered)[(position - jnp.arange(size)) % size]
+    return in_order(tiles, concat_dim)
 
 
 def phase(left_ids, right_ids, modulus, orient):
@@ -204,7 +227,7 @@
         canon = forward_rows(mine)
         mcount = canon.shape[0]
         sent = canon_to_groups(canon, row_count)
-        got = lax.all_to_all(sent, "row", split_axis=0, concat_axis=2, tiled=True)[0]
+        got = exchange_directly(sent, "row", 0, 2)[0]
         other = lax.ppermute(got, "wl", perm=[(0, 1), (1, 0)])
         got = got.reshape((2, row_count, own_rows, got.shape[-1]))
         other = other.reshape(got.shape)

time: 724 us -> 910 us (1.26)
  waiting for transfers between devices: 274 us -> 403 us
  starting transfers between devices: 24.9 us -> 80.9 us
    ppermute x0 -> x15, waiting for transfers between devices: none -> 159 us  [exchange_directly(): lax.ppermute(sent, axis, [(i, (i + lap) % size) for i in range(size)])]
    ppermute x0 -> x15, starting transfers between devices: none -> 59.6 us  [exchange_directly(): lax.ppermute(sent, axis, [(i, (i + lap) % size) for i in range(size)])]
    all_to_all x1 -> x0, waiting for transfers between devices: 32.1 us -> none  [local(): lax.all_to_all(sent, 'row', split_axis=0, concat_axis=2, tiled=True)[0]]
    unnamed x118 -> x112, local copies, waits for them, and re-layouts: 48.7 us -> 51.9 us
  transfers between devices with their start and end apart: 9 -> 23, of which waited for: 6 -> 16; matrix products, arithmetic and copies ran while one was open for 36% -> 27% of each run, Pallas kernels for 0% -> 0%
where the time goes in v1:
time: 910 us; the launch traced here: 903 us
  waiting for transfers between devices  403 us (44%)
  matrix products  179 us (20%)
  local copies, waits for them, and re-layouts  166 us (18%)
  starting transfers between devices  80.9 us (9%)
  other arithmetic  69.3 us (8%)
    ppermute x15, waiting for transfers between devices, exchange_directly(): lax.ppermute(sent, axis, [(i, (i + lap) % size) for i in range(size)])  159 us
    all_to_all x1, waiting for transfers between devices, local(): lax.all_to_all(summed, 'row', split_axis=1, concat_axis=1, tiled=True)  91.5 us
    ppermute x1, waiting for transfers between devices, local(): other = lax.ppermute(got, 'wl', perm=[(0, 1), (1, 0)])  82.2 us
    ppermute x15, starting transfers between devices, exchange_directly(): lax.ppermute(sent, axis, [(i, (i + lap) % size) for i in range(size)])  59.6 us
    dot_general x5, matrix products, inverse_cols_half(): jnp.einsum('fken,aenj->fkaj', second_tab, turned, precision=PRECISE)  54.1 us
    unnamed x112, local copies, waits for them, and re-layouts  51.9 us
    ppermute x4, waiting for transfers between devices, local(): incoming.append(lax.ppermute(given, 'wl', perm=[(0, 1), (1, 0)]))  41.1 us
    ppermute x1, waiting for transfers between devices, local(): taken = lax.ppermute(theirs, 'wl', perm=[(0, 1), (1, 0)])  29.8 us
  transfers between devices with their start and end apart: 23, of which 16 were waited for; matrix products, arithmetic and copies ran while one was open for 27% of the time, Pallas kernels for 0%

profile of v1, /device:TPU:10, one launch (start us, length us, event | category | flops | bytes accessed | tf_op | source)
XLA Modules:
  0.0 902.8 jit_solution(2297222661518572096)
XLA Ops:
  41.8 4.8 convolution_convert_fusion
  46.7 7.7 pad_maximum_fusion
  54.4 6.4 all-to-all-start
  65.5 6.8 fusion.46
  75.4 14.3 %fusion.17 = f32[2,32,128,2,64,1]{2,4,5,3,1,0:T(8,128)S(1)} fusion(f32[2,32,2,128,128,1]{4,1,3,0,2,5:T(8,128)S(1)} %maximum_bitcast_fusion.1, f32[1,2,2,64,128]{4,3,2,1,0:T(8,128)S(1)} %maximum_bitcast_fusion.22, f32[1,2,2,64,128]{4,3,2,1,0:T(8,128)S(1)} %maximum_bitcast_fusion.21), kind=kOutput, calls=%fused_computation.27 | convolution fusion | flops 3221291008 | bytes 12845056 | tf_op jit(solution)/shard_map/oaern,oenfk->oarfk/dot_general | solution.py:103
  97.0 5.4 copy.173
  116.3 44.4 %collective-permute-start.5 = (f32[1,2,128,256]{3,2,1,0:T(8,128)S(1)}, f32[1,2,128,256]{3,2,1,0:T(8,128)S(1)}, u32[]{:S(2)}, u32[]{:S(2)}) collective-permute-start(f32[1,2,128,256]{3,2,1,0:T(8,128)S(1)} %get-tuple-element.160), channel_id=1, source_target_pairs={{0,6},{1,7},{2,8},{3,9},{4,10},{5,11},{6,12},{7,13},{8,14},{9,15},... | collective-permute-start | bytes 786440 | tf_op jit(solution)/shard_map/ppermute | solution.py:29
  161.4 94.3 %collective-permute-done.1 = f32[1,2,128,256]{3,2,1,0:T(8,128)S(1)} collective-permute-done((f32[1,2,128,256]{3,2,1,0:T(8,128)S(1)}, f32[1,2,128,256]{3,2,1,0:T(8,128)S(1)}, u32[]{:S(2)}, u32[]{:S(2)}) %collective-permute-start.1) | collective-permute-done | bytes 262176 | tf_op jit(solution)/shard_map/ppermute | solution.py:29
  256.4 16.0 %collective-permute-done.2 = f32[1,2,128,256]{3,2,1,0:T(8,128)S(1)} collective-permute-done((f32[1,2,128,256]{3,2,1,0:T(8,128)S(1)}, f32[1,2,128,256]{3,2,1,0:T(8,128)S(1)}, u32[]{:S(2)}, u32[]{:S(2)}) %collective-permute-start.2) | collective-permute-done | bytes 262176 | tf_op jit(solution)/shard_map/ppermute | solution.py:29
  273.1 5.0 collective-permute-done.3
  281.0 8.4 collective-permute-done.4
  293.6 9.8 %collective-permute-done.5 = f32[1,2,128,256]{3,2,1,0:T(8,128)S(1)} collective-permute-done((f32[1,2,128,256]{3,2,1,0:T(8,128)S(1)}, f32[1,2,128,256]{3,2,1,0:T(8,128)S(1)}, u32[]{:S(2)}, u32[]{:S(2)}) %collective-permute-start.5) | collective-permute-done | bytes 262176 | tf_op jit(solution)/shard_map/ppermute | solution.py:29
  304.2 4.8 collective-permute-done.6
  309.0 5.0 collective-permute-start.11
  314.7 5.6 collective-permute-done.7
  321.0 7.2 collective-permute-done.8
  337.4 5.0 gather_fusion
  342.4 4.7 copy.175
  358.2 82.2 %collective-permute-done.15 = f32[2,2048,256]{2,1,0:T(8,128)} collective-permute-done((f32[2,2048,256]{2,1,0:T(8,128)}, f32[2,2048,256]{2,1,0:T(8,128)}, u32[]{:S(2)}, u32[]{:S(2)}) %collective-permute-start.15) | collective-permute-done | bytes 4194336 | tf_op jit(solution)/shard_map/ppermute | solution.py:231
  445.5 10.0 %copy.178 = f32[2,16,2,128,256]{4,2,1,0,3:T(2,128)} copy(f32[2,16,2,128,256]{4,3,0,1,2:T(8,128)S(1)} %pad_maximum_fusion.1) | data formatting | bytes 16777216 | tf_op jit(solution)/shard_map/stack | solution.py:236
  455.5 10.9 %reshape.2242 = f32[2,32,128,256,1,1]{3,1,0,2,4,5:T(8,128)} reshape(f32[2,16,2,128,256]{4,2,1,0,3:T(2,128)} %copy.178) | data formatting | bytes 16777216 | tf_op jit(solution)/shard_map/reshape;reshape | solution.py:117
  466.4 16.7 %fusion.19 = f32[2,32,2,128,256]{4,1,3,2,0:T(8,128)S(1)} fusion(f32[2,32,128,256,1,1]{3,1,0,2,4,5:T(8,128)} %reshape.2242, f32[1,2,2,32,32]{4,3,2,1,0:T(8,128)S(1)} %fusion.98, f32[1,2,2,32,32]{4,3,2,1,0:T(8,128)S(1)} %maximum_bitcast_fusion.31), kind=kOutput, calls=%fused_computation.31 | convolution fusion | flops 3221233664 | bytes 25198592 | tf_op jit(solution)/shard_map/oafeb,ebnj->oafnj/dot_general | solution.py:119
  483.1 5.5 subtract_bitcast_fusion
  488.6 5.1 maximum_bitcast_fusion
  493.7 25.5 %fusion.22 = f32[2,2,128,32,256]{4,2,3,1,0:T(8,128)S(1)} fusion(f32[2,32,2,128,256,1]{4,1,3,0,2,5:T(8,128)S(1)} %maximum_bitcast_fusion, f32[1,2,2,128,128]{4,3,2,1,0:T(8,128)} %maximum_bitcast_fusion.12, f32[1,2,2,128,128]{4,3,2,1,0:T(8,128)} %maximum_bitcast_fusion.11), kind=kOutput, calls=%fused_computation.32 | convolution fusion | flops 12885032960 | bytes 34078720 | tf_op jit(solution)/shard_map/ofekn,oaenj->ofkaj/dot_general | solution.py:129
  519.2 5.8 copy-done.3
  529.3 8.2 copy.184
  541.6 4.4 copy.183
  554.8 11.5 %copy.168 = bf16[1,2,2,16,256,256]{5,4,3,2,1,0:T(8,128)(2,1)} copy(bf16[1,2,2,16,256,256]{4,5,2,1,3,0:T(8,128)(2,1)} %bitcast.54) | data formatting | bytes 16777216 | tf_op jit(solution)/shard_map/all_to_all | solution.py:245
  566.2 10.8 %fusion.32 = (f32[1,4096,256]{2,1,0:T(8,128)S(1)}, f32[1,4096,256]{2,1,0:T(8,128)S(1)}) fusion(bf16[2,2,4096,256]{3,2,1,0:T(8,128)(2,1)} %bitcast.642, f32[]{:T(128)} %bitcast.157, f32[]{:T(128)} %bitcast.156, f32[2,4096,256]{2,1,0:T(8,128)} %maximum_select_fusion, f32[1,1,128,32,256]{4,3,2,1,0:T(8,128)} %copy.183, f32[]{:T(128)} %bitcast.162, f32[]{:T(128)} %bitcast.161, ...), kind=kLoop, calls=%fused_computation.50 | loop fusion | flops 36700160 | bytes 33554448 | tf_op jit(solution)/shard_map/sub | solution.py:267
  582.0 7.9 fusion.47
  593.1 9.4 %fusion.57 = f32[2,16,32,256]{3,1,2,0:T(8,128)S(1)} fusion(f32[32,2,128,256]{3,0,2,1:T(8,128)S(1)} %pad_maximum_fusion.2, f32[1,2,16,128]{3,2,1,0:T(8,128)S(1)} %copy-done.18, f32[1,2,16,128]{3,2,1,0:T(8,128)S(1)} %copy-done.17), kind=kOutput, calls=%fused_computation.112 | convolution fusion | flops 805314560 | bytes 9469952 | tf_op jit(solution)/shard_map/fken,aenj->fkaj/dot_general | solution.py:148
  604.0 10.5 %fusion.60 = f32[2,16,32,256]{3,1,2,0:T(8,128)} fusion(f32[32,2,128,256]{3,0,2,1:T(8,128)S(1)} %pad_maximum_fusion.2, f32[1,2,16,128]{3,2,1,0:T(8,128)S(1)} %copy-done.16, f32[1,2,16,128]{3,2,1,0:T(8,128)S(1)} %get-tuple-element.195), kind=kOutput, calls=%fused_computation.113 | convolution fusion | flops 805314560 | bytes 9469952 | tf_op jit(solution)/shard_map/fken,aenj->fkaj/dot_general | solution.py:148
  615.1 10.5 %fusion.63 = f32[2,16,32,256]{3,1,2,0:T(8,128)} fusion(f32[32,2,128,256]{3,0,2,1:T(8,128)S(1)} %pad_maximum_fusion.2, f32[1,2,16,128]{3,2,1,0:T(8,128)S(1)} %copy-done.22, f32[1,2,16,128]{3,2,1,0:T(8,128)S(1)} %copy-done.21), kind=kOutput, calls=%fused_computation.114 | convolution fusion | flops 805314560 | bytes 9469952 | tf_op jit(solution)/shard_map/fken,aenj->fkaj/dot_general | solution.py:148
  627.1 10.7 %fusion.66 = f32[2,16,32,256]{3,1,2,0:T(8,128)} fusion(f32[32,2,128,256]{3,0,2,1:T(8,128)S(1)} %pad_maximum_fusion.2, f32[1,2,16,128]{3,2,1,0:T(8,128)S(1)} %copy-done.20, f32[1,2,16,128]{3,2,1,0:T(8,128)S(1)} %copy-done.19), kind=kOutput, calls=%fused_computation.115 | convolution fusion | flops 805314560 | bytes 9469952 | tf_op jit(solution)/shard_map/fken,aenj->fkaj/dot_general | solution.py:148
  638.7 13.0 %fusion.48 = f32[2,64,32,256]{3,1,2,0:T(8,128)S(1)} fusion(f32[32,2,128,256]{3,0,2,1:T(8,128)} %copy-done.2, f32[1,2,64,128]{3,2,1,0:T(8,128)S(1)} %get-tuple-element.180, f32[1,2,64,128]{3,2,1,0:T(8,128)S(1)} %get-tuple-element.179), kind=kOutput, calls=%fused_computation.93 | convolution fusion | flops 3221258240 | bytes 12713984 | tf_op jit(solution)/shard_map/fken,aenj->fkaj/dot_general | solution.py:148
  654.2 19.3 %collective-permute-done.18 = f32[2,16,32,256]{3,1,2,0:T(8,128)} collective-permute-done((f32[2,16,32,256]{3,1,2,0:T(8,128)}, f32[2,16,32,256]{3,1,2,0:T(8,128)}, u32[]{:S(2)}, u32[]{:S(2)}) %collective-permute-start.18) | collective-permute-done | bytes 1048608 | tf_op jit(solution)/shard_map/ppermute | solution.py:283
  673.5 21.8 %collective-permute-done.19 = f32[2,16,32,256]{3,1,2,0:T(8,128)} collective-permute-done((f32[2,16,32,256]{3,1,2,0:T(8,128)}, f32[2,16,32,256]{3,1,2,0:T(8,128)}, u32[]{:S(2)}, u32[]{:S(2)}) %collective-permute-start.19) | collective-permute-done | bytes 1048608 | tf_op jit(solution)/shard_map/ppermute | solution.py:283
  695.4 5.8 maximum_add_fusion
  705.6 7.7 all-to-all-start.1
  714.1 91.5 %all-to-all-done.1 = f32[2,16,128,256]{3,2,0,1:T(8,128)} async-done(((f32[2,16,128,256]{3,2,0,1:T(8,128)}), f32[2,16,128,256]{3,2,0,1:T(8,128)}, u32[]{:S(2)}, u32[]{:S(2)}) %all-to-all-start.1) | async-done | bytes 4194336 | tf_op jit(solution)/shard_map/all_to_all | solution.py:292
  805.7 18.1 %convolution_bitcast_fusion = f32[2,32,2,128,256]{4,1,3,2,0:T(8,128)S(1)} fusion(f32[2,16,128,256,1,1]{3,2,0,1,5,4:T(8,128)} %bitcast.213, f32[1,2,2,32,16]{3,4,2,1,0:T(8,128)S(1)} %maximum_bitcast_fusion.45, f32[1,2,2,32,16]{3,4,2,1,0:T(8,128)S(1)} %maximum_bitcast_fusion.44), kind=kOutput, calls=%fused_computation.33 | convolution fusion | flops 1610616832 | bytes 20987904 | tf_op jit(solution)/shard_map/oafem,emRj->oafRj/dot_general | solution.py:170
  829.8 6.9 fusion.38
  836.7 7.1 fusion.51
  847.1 8.1 fusion.40
  855.2 6.9 fusion.52
  863.3 29.8 %collective-permute-done.20 = f32[2,128,2048]{1,2,0:T(8,128)} collective-permute-done((f32[2,128,2048]{1,2,0:T(8,128)S(1)}, f32[2,128,2048]{1,2,0:T(8,128)}, u32[]{:S(2)}, u32[]{:S(2)}) %collective-permute-start.20) | collective-permute-done | bytes 2097184 | tf_op jit(solution)/shard_map/ppermute | solution.py:296
  897.2 5.3 copy.205
  (259 shorter events, 156.2 us)
Async XLA Ops:
  0.0 348.8 %copy-start = (f32[4,2]{0,1:T(2,128)S(1)}, f32[4,2]{0,1:T(2,128)}, u32[]{:S(2)}) copy-start(f32[4,2]{0,1:T(2,128)} %param.23) | copy-start | bytes 100
  0.0 41.8 %copy-start.23 = (pred[128]{0:T(512)(128)(4,1)}, pred[128]{0:T(512)(128)(4,1)S(1)}, u32[]{:S(2)}) copy-start(pred[128]{0:T(512)(128)(4,1)S(1)} %get-tuple-element.246) | copy-start | bytes 388
  22.2 8.8 copy-start.9
  23.3 8.4 copy-start.10
  23.3 9.1 %copy-start.8 = (bf16[2,2,256,128]{2,3,1,0:T(8,128)(2,1)S(1)}, bf16[2,2,256,128]{2,3,1,0:T(8,128)(2,1)}, u32[]{:S(2)}) copy-start(bf16[2,2,256,128]{2,3,1,0:T(8,128)(2,1)} %copy.262) | copy-start | bytes 786436
  54.4 500.4 %all-to-all-start = ((bf16[16,2,2,256,256]{3,4,2,1,0:T(8,128)(2,1)}), bf16[16,2,2,256,256]{3,4,2,1,0:T(8,128)(2,1)}, u32[]{:S(2)}, u32[]{:S(2)}) async-start(bf16[16,2,2,256,256]{3,4,2,1,0:T(8,128)(2,1)} %pad_maximum_fusion), calls=%async_computation | async-start | bytes 16777216 | tf_op jit(solution)/shard_map/all_to_all | solution.py:245
  89.7 3.1 copy-start.25
  92.2 2.6 copy-start.7
  108.4 7.9 collective-permute-start
  108.5 147.2 %collective-permute-start.1 = (f32[1,2,128,256]{3,2,1,0:T(8,128)S(1)}, f32[1,2,128,256]{3,2,1,0:T(8,128)S(1)}, u32[]{:S(2)}, u32[]{:S(2)}) collective-permute-start(f32[1,2,128,256]{3,2,1,0:T(8,128)S(1)} %get-tuple-element.164), channel_id=1, source_target_pairs={{0,2},{1,3},{2,4},{3,5},{4,6},{5,7},{6,8},{7,9},{8,10},{9,11},{10,... | collective-permute-start | bytes 786440 | tf_op jit(solution)/shard_map/ppermute | solution.py:29
  110.0 162.4 %collective-permute-start.2 = (f32[1,2,128,256]{3,2,1,0:T(8,128)S(1)}, f32[1,2,128,256]{3,2,1,0:T(8,128)S(1)}, u32[]{:S(2)}, u32[]{:S(2)}) collective-permute-start(f32[1,2,128,256]{3,2,1,0:T(8,128)S(1)} %get-tuple-element.163), channel_id=1, source_target_pairs={{0,3},{1,4},{2,5},{3,6},{4,7},{5,8},{6,9},{7,10},{8,11},{9,12},{10... | collective-permute-start | bytes 786440 | tf_op jit(solution)/shard_map/ppermute | solution.py:29
  112.2 166.0 %collective-permute-start.3 = (f32[1,2,128,256]{3,2,1,0:T(8,128)S(1)}, f32[1,2,128,256]{3,2,1,0:T(8,128)S(1)}, u32[]{:S(2)}, u32[]{:S(2)}) collective-permute-start(f32[1,2,128,256]{3,2,1,0:T(8,128)S(1)} %get-tuple-element.162), channel_id=1, source_target_pairs={{0,4},{1,5},{2,6},{3,7},{4,8},{5,9},{6,10},{7,11},{8,12},{9,13},{1... | collective-permute-start | bytes 786440 | tf_op jit(solution)/shard_map/ppermute | solution.py:29
  112.5 176.9 %collective-permute-start.4 = (f32[1,2,128,256]{3,2,1,0:T(8,128)S(1)}, f32[1,2,128,256]{3,2,1,0:T(8,128)S(1)}, u32[]{:S(2)}, u32[]{:S(2)}) collective-permute-start(f32[1,2,128,256]{3,2,1,0:T(8,128)S(1)} %get-tuple-element.161), channel_id=1, source_target_pairs={{0,5},{1,6},{2,7},{3,8},{4,9},{5,10},{6,11},{7,12},{8,13},{9,14},{... | collective-permute-start | bytes 786440 | tf_op jit(solution)/shard_map/ppermute | solution.py:29
  116.3 187.2 %collective-permute-start.5 = (f32[1,2,128,256]{3,2,1,0:T(8,128)S(1)}, f32[1,2,128,256]{3,2,1,0:T(8,128)S(1)}, u32[]{:S(2)}, u32[]{:S(2)}) collective-permute-start(f32[1,2,128,256]{3,2,1,0:T(8,128)S(1)} %get-tuple-element.160), channel_id=1, source_target_pairs={{0,6},{1,7},{2,8},{3,9},{4,10},{5,11},{6,12},{7,13},{8,14},{9,15},... | collective-permute-start | bytes 786440 | tf_op jit(solution)/shard_map/ppermute | solution.py:29
  255.7 53.3 %collective-permute-start.6 = (f32[1,2,128,256]{3,2,1,0:T(8,128)S(1)}, f32[1,2,128,256]{3,2,1,0:T(8,128)S(1)}, u32[]{:S(2)}, u32[]{:S(2)}) collective-permute-start(f32[1,2,128,256]{3,2,1,0:T(8,128)S(1)} %get-tuple-element.159), channel_id=1, source_target_pairs={{0,7},{1,8},{2,9},{3,10},{4,11},{5,12},{6,13},{7,14},{8,15},{9,0},... | collective-permute-start | bytes 786440 | tf_op jit(solution)/shard_map/ppermute | solution.py:29
  272.4 47.9 %collective-permute-start.7 = (f32[1,2,128,256]{3,2,1,0:T(8,128)S(1)}, f32[1,2,128,256]{3,2,1,0:T(8,128)S(1)}, u32[]{:S(2)}, u32[]{:S(2)}) collective-permute-start(f32[1,2,128,256]{3,2,1,0:T(8,128)S(1)} %get-tuple-element.158), channel_id=1, source_target_pairs={{0,8},{1,9},{2,10},{3,11},{4,12},{5,13},{6,14},{7,15},{8,0},{9,1},... | collective-permute-start | bytes 786440 | tf_op jit(solution)/shard_map/ppermute | solution.py:29
  278.2 50.1 %collective-permute-start.8 = (f32[1,2,128,256]{3,2,1,0:T(8,128)S(1)}, f32[1,2,128,256]{3,2,1,0:T(8,128)S(1)}, u32[]{:S(2)}, u32[]{:S(2)}) collective-permute-start(f32[1,2,128,256]{3,2,1,0:T(8,128)S(1)} %get-tuple-element.157), channel_id=1, source_target_pairs={{0,9},{1,10},{2,11},{3,12},{4,13},{5,14},{6,15},{7,0},{8,1},{9,2},... | collective-permute-start | bytes 786440 | tf_op jit(solution)/shard_map/ppermute | solution.py:29
  289.4 39.6 %collective-permute-start.9 = (f32[1,2,128,256]{3,2,1,0:T(8,128)S(1)}, f32[1,2,128,256]{3,2,1,0:T(8,128)S(1)}, u32[]{:S(2)}, u32[]{:S(2)}) collective-permute-start(f32[1,2,128,256]{3,2,1,0:T(8,128)S(1)} %get-tuple-element.156), channel_id=1, source_target_pairs={{0,10},{1,11},{2,12},{3,13},{4,14},{5,15},{6,0},{7,1},{8,2},{9,3},... | collective-permute-start | bytes 786440 | tf_op jit(solution)/shard_map/ppermute | solution.py:29
  303.4 26.3 %collective-permute-start.10 = (f32[1,2,128,256]{3,2,1,0:T(8,128)S(1)}, f32[1,2,128,256]{3,2,1,0:T(8,128)S(1)}, u32[]{:S(2)}, u32[]{:S(2)}) collective-permute-start(f32[1,2,128,256]{3,2,1,0:T(8,128)S(1)} %get-tuple-element.155), channel_id=1, source_target_pairs={{0,11},{1,12},{2,13},{3,14},{4,15},{5,0},{6,1},{7,2},{8,3},{9,4},{... | collective-permute-start | bytes 786440 | tf_op jit(solution)/shard_map/ppermute | solution.py:29
  309.0 21.5 %collective-permute-start.11 = (f32[1,2,128,256]{3,2,1,0:T(8,128)S(1)}, f32[1,2,128,256]{3,2,1,0:T(8,128)S(1)}, u32[]{:S(2)}, u32[]{:S(2)}) collective-permute-start(f32[1,2,128,256]{3,2,1,0:T(8,128)S(1)} %get-tuple-element.154), channel_id=1, source_target_pairs={{0,12},{1,13},{2,14},{3,15},{4,0},{5,1},{6,2},{7,3},{8,4},{9,5},{1... | collective-permute-start | bytes 786440 | tf_op jit(solution)/shard_map/ppermute | solution.py:29
  320.3 10.9 %collective-permute-start.12 = (f32[1,2,128,256]{3,2,1,0:T(8,128)S(1)}, f32[1,2,128,256]{3,2,1,0:T(8,128)S(1)}, u32[]{:S(2)}, u32[]{:S(2)}) collective-permute-start(f32[1,2,128,256]{3,2,1,0:T(8,128)S(1)} %get-tuple-element.153), channel_id=1, source_target_pairs={{0,13},{1,14},{2,15},{3,0},{4,1},{5,2},{6,3},{7,4},{8,5},{9,6},{10... | collective-permute-start | bytes 786440 | tf_op jit(solution)/shard_map/ppermute | solution.py:29
  328.3 7.3 collective-permute-start.13
  329.0 7.7 collective-permute-start.14
  347.1 93.3 %collective-permute-start.15 = (f32[2,2048,256]{2,1,0:T(8,128)}, f32[2,2048,256]{2,1,0:T(8,128)}, u32[]{:S(2)}, u32[]{:S(2)}) collective-permute-start(f32[2,2048,256]{2,1,0:T(8,128)} %bitcast.141), channel_id=1, source_target_pairs={{0,16},{16,0},{1,17},{17,1},{2,18},{18,2},{3,19},{19,3},{4,20},{20... | collective-permute-start | bytes 12582920 | tf_op jit(solution)/shard_map/ppermute | solution.py:231
  352.0 3.6 copy-start.12
  352.0 3.6 copy-start.14
  519.2 5.8 copy-start.3
  582.0 8.0 copy-start.11
  591.4 1.7 copy-start.17
  591.4 1.7 copy-start.18
  593.0 34.1 %copy-start.2 = (f32[32,2,128,256]{3,0,2,1:T(8,128)}, f32[32,2,128,256]{3,0,2,1:T(8,128)S(1)}, u32[]{:S(2)}) copy-start(f32[32,2,128,256]{3,0,2,1:T(8,128)S(1)} %pad_maximum_fusion.2) | copy-start | bytes 25165828
  593.1 11.0 %copy-start.16 = (f32[1,2,16,128]{3,2,1,0:T(8,128)S(1)}, f32[1,2,16,128]{3,2,1,0:T(8,128)}, u32[]{:S(2)}) copy-start(f32[1,2,16,128]{3,2,1,0:T(8,128)} %get-tuple-element.196) | copy-start | bytes 49156
  602.4 51.8 %collective-permute-start.16 = (f32[2,16,32,256]{3,1,2,0:T(8,128)S(1)}, f32[2,16,32,256]{3,1,2,0:T(8,128)S(1)}, u32[]{:S(2)}, u32[]{:S(2)}) collective-permute-start(f32[2,16,32,256]{3,1,2,0:T(8,128)S(1)} %fusion.57), channel_id=1, source_target_pairs={{0,16},{16,0},{1,17},{17,1},{2,18},{18,2},{3,19},{19,3},{4,20},{20... | collective-permute-start | bytes 3145736 | tf_op jit(solution)/shard_map/ppermute | solution.py:283
  604.0 11.0 %copy-start.21 = (f32[1,2,16,128]{3,2,1,0:T(8,128)S(1)}, f32[1,2,16,128]{3,2,1,0:T(8,128)}, u32[]{:S(2)}) copy-start(f32[1,2,16,128]{3,2,1,0:T(8,128)} %get-tuple-element.197) | copy-start | bytes 49156
  604.0 11.0 %copy-start.22 = (f32[1,2,16,128]{3,2,1,0:T(8,128)S(1)}, f32[1,2,16,128]{3,2,1,0:T(8,128)}, u32[]{:S(2)}) copy-start(f32[1,2,16,128]{3,2,1,0:T(8,128)} %get-tuple-element.198) | copy-start | bytes 49156
  614.5 39.7 %collective-permute-start.17 = (f32[2,16,32,256]{3,1,2,0:T(8,128)}, f32[2,16,32,256]{3,1,2,0:T(8,128)S(1)}, u32[]{:S(2)}, u32[]{:S(2)}) collective-permute-start(f32[2,16,32,256]{3,1,2,0:T(8,128)} %fusion.60), channel_id=1, source_target_pairs={{0,16},{16,0},{1,17},{17,1},{2,18},{18,2},{3,19},{19,3},{4,20},{20... | collective-permute-start | bytes 3145736 | tf_op jit(solution)/shard_map/ppermute | solution.py:283
  615.1 12.0 %copy-start.19 = (f32[1,2,16,128]{3,2,1,0:T(8,128)S(1)}, f32[1,2,16,128]{3,2,1,0:T(8,128)}, u32[]{:S(2)}) copy-start(f32[1,2,16,128]{3,2,1,0:T(8,128)} %get-tuple-element.199) | copy-start | bytes 49156
  615.1 12.0 %copy-start.20 = (f32[1,2,16,128]{3,2,1,0:T(8,128)S(1)}, f32[1,2,16,128]{3,2,1,0:T(8,128)}, u32[]{:S(2)}) copy-start(f32[1,2,16,128]{3,2,1,0:T(8,128)} %get-tuple-element.200) | copy-start | bytes 49156
  625.6 48.0 %collective-permute-start.18 = (f32[2,16,32,256]{3,1,2,0:T(8,128)}, f32[2,16,32,256]{3,1,2,0:T(8,128)}, u32[]{:S(2)}, u32[]{:S(2)}) collective-permute-start(f32[2,16,32,256]{3,1,2,0:T(8,128)} %fusion.63), channel_id=1, source_target_pairs={{0,16},{16,0},{1,17},{17,1},{2,18},{18,2},{3,19},{19,3},{4,20},{20... | collective-permute-start | bytes 3145736 | tf_op jit(solution)/shard_map/ppermute | solution.py:283
  637.8 57.6 %collective-permute-start.19 = (f32[2,16,32,256]{3,1,2,0:T(8,128)}, f32[2,16,32,256]{3,1,2,0:T(8,128)}, u32[]{:S(2)}, u32[]{:S(2)}) collective-permute-start(f32[2,16,32,256]{3,1,2,0:T(8,128)} %fusion.66), channel_id=1, source_target_pairs={{0,16},{16,0},{1,17},{17,1},{2,18},{18,2},{3,19},{19,3},{4,20},{20... | collective-permute-start | bytes 3145736 | tf_op jit(solution)/shard_map/ppermute | solution.py:283
  705.6 100.1 %all-to-all-start.1 = ((f32[2,16,128,256]{3,2,0,1:T(8,128)}), f32[2,16,128,256]{3,2,0,1:T(8,128)}, u32[]{:S(2)}, u32[]{:S(2)}) async-start(f32[2,16,128,256]{3,2,0,1:T(8,128)} %copy.197), calls=%async_computation.1 | async-start | bytes 8388608 | tf_op jit(solution)/shard_map/all_to_all | solution.py:292
  823.8 0.7 copy-start.15
  824.5 1.8 copy-start.24
  828.7 8.1 copy-start.4
  829.8 14.0 %copy-start.6 = (f32[32,2,128,128,1]{3,0,2,1,4:T(8,128)}, f32[32,2,128,128,1]{3,0,2,1,4:T(8,128)S(1)}, u32[]{:S(2)}) copy-start(f32[32,2,128,128,1]{3,0,2,1,4:T(8,128)S(1)} %maximum_bitcast_fusion.5) | copy-start | bytes 12582916
  845.0 48.0 %collective-permute-start.20 = (f32[2,128,2048]{1,2,0:T(8,128)S(1)}, f32[2,128,2048]{1,2,0:T(8,128)}, u32[]{:S(2)}, u32[]{:S(2)}) collective-permute-start(f32[2,128,2048]{1,2,0:T(8,128)S(1)} %bitcast.651), channel_id=1, source_target_pairs={{0,16},{16,0},{1,17},{17,1},{2,18},{18,2},{3,19},{19,3},{4,20},{20... | collective-permute-start | bytes 6291464 | tf_op jit(solution)/shard_map/ppermute | solution.py:296
  846.6 8.5 copy-start.5
  894.9 7.6 copy-start.1
  (1 other events, 0.7 us)
